TPU v7x, 32 devices: a whole 2x2x4 slice. The times are simulated.
32 devices in a mesh: groups: 2 (over y), blk: 4 (over z), pool: 4 (over x, core).
Axes of the slice: x: 2, y: 2, z: 4, core: 2. Of those that a mesh axis runs over, the one named last changes fastest.
Arguments:
- q_new: bfloat16 [1024, 8192], P(('groups', 'blk'), 'pool'), parts along dimension 0, may hold values from -64 to 64
- kv_new: bfloat16 [1024, 8, 256], P(('groups', 'blk'), 'pool'), parts along dimension 0, may hold values from -7 to 7
- kv_cache: bfloat16 [256, 8, 128, 256], P(('groups', 'blk'), 'pool'), parts along dimension 0, may hold values from -4.5 to 4.5
- page_table: int32 [16], P('groups'), parts along dimension 0, may hold values from 0 to 127, as said below
- block_offsets: int32 [8], P('groups'), parts along dimension 0, may hold values from 0 to 3, each once
Outputs:
- attended: bfloat16 [1024, 8192], P(('groups', 'blk'), 'pool'), parts along dimension 0
There are 2 independent parts, one for each index of `groups`. A program takes and returns all parts, laid end to end along the dimension named above; each array names one. Nothing has to cross between parts.
Inputs may be any that keep to these rules, and one draw needn't show every extreme that they name: `page_table`: distinct slots; slot s lies on blk index s // 32; at most 4 entries lie on the slots of one blk index, and exactly 4 on some blk index.
All inputs are finite; a program needn't handle non-finite values.
Results may differ from a plain program's by a relative error of at most 0.0045.
Values may be sent and summed in bfloat16 or wider, within the bound.
No kernel may reach another device: no remote copies, remote signals or barrier semaphores. Data moves between devices by JAX's collectives and lax.ppermute only.
A program may use at most 64 MiB of HBM per device.

v0:
```python
import math
import jax
import jax.numpy as jnp
from jax import lax
from jax.sharding import PartitionSpec as P

PG = 2
CAP = 4


def divisor_below(total_count, upper_limit):
    for candidate in range(min(total_count, upper_limit), 0, -1):
        if total_count % candidate == 0:
            return candidate
    return 1


def attend(running, queries, entries, visible, head_size):
    maxima, totals, summed = running
    score_scale = 1.0 / math.sqrt(head_size)
    scores = (
        jnp.einsum(
            "gqd,gkd->gqk", queries, entries[..., :head_size], preferred_element_type=jnp.float32
        )
        * score_scale
    )
    scores = jnp.where(visible[None], scores, -1e30)
    row_top = jnp.maximum(maxima, jnp.max(scores, axis=2))
    factor = jnp.exp(maxima - row_top)
    weights = jnp.where(visible[None], jnp.exp(scores - row_top[..., None]), 0.0)
    totals = totals * factor + jnp.sum(weights, axis=2)
    summed = summed * factor[..., None] + jnp.einsum(
        "gqk,gkd->gqd",
        weights.astype(jnp.bfloat16),
        entries[..., head_size:],
        preferred_element_type=jnp.float32,
    )
    return (row_top, totals, summed)


def local(q_new, kv_new, kv_cache, page_table, block_offsets):
    q_rows = q_new.shape[0]
    kv_heads = kv_new.shape[1]
    head_size = kv_new.shape[2] // 2
    group_size = q_new.shape[1] // (head_size * kv_heads)
    slots_dev = kv_cache.shape[0]
    page_len = kv_cache.shape[2]
    blocks = lax.axis_size("blk")
    myself = lax.axis_index("blk")
    block_ids = jnp.arange(blocks, dtype=jnp.int32)
    my_offset = jnp.sum(jnp.where(block_ids == myself, block_offsets, 0))
    query_pos = jnp.tile(my_offset * q_rows + jnp.arange(q_rows, dtype=jnp.int32), group_size)
    queries = (
        q_new.reshape(q_rows, kv_heads, group_size, head_size)
        .transpose(1, 2, 0, 3)
        .reshape(kv_heads, group_size * q_rows, head_size)
    )
    query_span = group_size * q_rows
    running = (
        jnp.full((kv_heads, query_span), -1e30, jnp.float32),
        jnp.zeros((kv_heads, query_span), jnp.float32),
        jnp.zeros((kv_heads, query_span, head_size), jnp.float32),
    )
    carried = running
    incoming = lax.all_gather(kv_new, "blk", axis=0, tiled=True)
    row_count = incoming.shape[0]
    block_rows = divisor_below(row_count, 512)
    parted = incoming.reshape(
        row_count // block_rows, block_rows, kv_heads, 2 * head_size
    ).transpose(0, 2, 1, 3)
    row_index = jnp.arange(row_count, dtype=jnp.int32).reshape(row_count // block_rows, block_rows)

    def visit_block(state_now, block_pair):
        entries, indices = block_pair
        source = indices // q_rows
        offsets = jnp.sum(
            jnp.where(source[:, None] == block_ids[None, :], block_offsets[None, :], 0), axis=1
        )
        key_pos = offsets * q_rows + indices % q_rows
        visible = key_pos[None, :] <= query_pos[:, None]
        return (attend(state_now, queries, entries, visible, head_size), None)

    carried, unused = lax.scan(visit_block, carried, (parted, row_index))
    running = carried
    page_owner = page_table // slots_dev
    owned = page_owner == myself
    page_rank = jnp.cumsum(owned.astype(jnp.int32)) - 1
    local_slot = page_table % slots_dev
    counts = jnp.sum((page_owner[None, :] == block_ids[:, None]).astype(jnp.int32), axis=1)
    per_peer = (CAP + blocks - 1) // blocks
    starts = jnp.cumsum(counts) - counts
    my_start = jnp.sum(jnp.where(block_ids == myself, starts, 0))
    peer_slots = jnp.arange(per_peer, dtype=jnp.int32)[None, :]
    wanted = (block_ids[:, None] - my_start) % blocks + peer_slots * blocks
    picked = owned[None, None, :] & (page_rank[None, None, :] == wanted[..., None])
    chosen = jnp.sum(jnp.where(picked, local_slot[None, None, :], 0), axis=2).reshape(-1)
    received = lax.all_to_all(kv_cache[chosen], "blk", split_axis=0, concat_axis=0, tiled=True)
    arriving = (myself - starts[:, None]) % blocks + peer_slots * blocks
    present = (arriving < counts[:, None]).reshape(-1)
    order_rank = jnp.cumsum(present.astype(jnp.int32)) - 1
    choose = present[None, :] & (order_rank[None, :] == jnp.arange(PG, dtype=jnp.int32)[:, None])
    positions = jnp.sum(
        jnp.where(choose, jnp.arange(blocks * per_peer, dtype=jnp.int32)[None, :], 0), axis=1
    )
    compact = received[positions]
    valid_all = jnp.ones((blocks * PG,), jnp.bool_)
    carried = running
    incoming = lax.all_gather(compact, "blk", axis=0, tiled=True)
    page_count = incoming.shape[0]
    group_pages = divisor_below(page_count, max(1, 512 // page_len))
    parted = incoming.reshape(
        page_count // group_pages, group_pages, kv_heads, page_len, 2 * head_size
    )
    parted = parted.transpose(0, 2, 1, 3, 4).reshape(
        page_count // group_pages, kv_heads, group_pages * page_len, 2 * head_size
    )
    flags = valid_all.reshape(page_count // group_pages, group_pages)

    def visit_pages(state_now, block_pair):
        entries, present = block_pair
        visible = jnp.repeat(present, page_len)[None, :]
        return (attend(state_now, queries, entries, visible, head_size), None)

    carried, unused = lax.scan(visit_pages, carried, (parted, flags))
    running = carried
    maxima, totals, summed = running
    attended = (summed / totals[..., None]).astype(jnp.bfloat16)
    attended = attended.reshape(kv_heads, group_size, q_rows, head_size).transpose(2, 0, 1, 3)
    return attended.reshape(q_rows, kv_heads * group_size * head_size)


def solution(mesh):
    return jax.shard_map(
        local,
        mesh=mesh,
        in_specs=(
            P(("groups", "blk"), "pool"),
            P(("groups", "blk"), "pool", None),
            P(("groups", "blk"), "pool", None, None),
            P("groups"),
            P("groups"),
        ),
        out_specs=P(("groups", "blk"), "pool"),
        check_vma=False,
    )
```

profile of v0, /device:TPU:0, one launch (start us, length us, event | category | flops | bytes accessed | tf_op | source)
XLA Modules:
  0.0 93.6 jit_solution(7782781215370035208)
XLA Ops:
  6.5 0.7 and_select_fusion.3
  7.2 0.7 convert_bitcast_fusion
  7.9 0.2 reduce-window.21
  8.1 0.1 convert_reduce_fusion
  8.2 0.2 reduce-window.22
  8.3 1.4 %fusion.36 = (s32[]{:T(128)}, s32[]{:T(128)}) fusion(s32[4]{0:T(128)} %param.11, s32[]{:T(128)S(6)} %axis_index.15, s32[4]{0:T(128)S(1)} %convert_reduce_fusion, s32[4,1]{0,1:T(1,128)S(1)} %reduce-window.22), kind=kLoop, calls=%fused_computation.76 | loop fusion | flops 22 | bytes 60 | tf_op jit(solution)/shard_map/reduce_sum | solution.py:51
  9.7 0.7 and_select_fusion.4
  10.4 0.2 select_reduce_fusion.1
  10.6 3.6 %gather_fusion = bf16[4,2,128,256]{3,2,1,0:T(8,128)(2,1)} fusion(bf16[32,2,128,256]{3,2,1,0:T(8,128)(2,1)} %param.9, s32[1024]{0:T(1024)S(1)} %pad_clamp_fusion.1), kind=kCustom, calls=%fused_computation | custom fusion | bytes 1048592 | tf_op jit(solution)/shard_map/gather | solution.py:97
  14.1 6.3 %all-to-all-start = ((bf16[4,2,128,256]{3,2,1,0:T(8,128)(2,1)}), bf16[4,2,128,256]{3,2,1,0:T(8,128)(2,1)S(1)}, u32[]{:S(2)}, u32[]{:S(2)}) async-start(bf16[4,2,128,256]{3,2,1,0:T(8,128)(2,1)} %gather_fusion), calls=%async_computation | async-start | bytes 1048576 | tf_op jit(solution)/shard_map/all_to_all | solution.py:97
  20.5 0.0 all-gather.3.cloned.1.call-start
  20.5 0.2 reduce-window.23
  20.7 0.1 fusion.34
  20.8 0.7 select_reduce_fusion
  21.6 0.9 copy.20
  22.5 22.8 %all_gather.6 = bf16[512,2,256]{2,0,1:T(8,128)(2,1)S(1)} all-gather(bf16[128,2,256]{2,0,1:T(8,128)(2,1)S(1)} %copy.20), channel_id=1, replica_groups=mesh['groups'=2,'blk'=4,'pool'=4] {'blk'}, dimensions={0}, use_global_device_ids=true | all-gather | bytes 655360 | tf_op jit(solution)/shard_map/all_gather | solution.py:65
  45.3 1.1 %copy.26 = bf16[16,8,16,128]{3,2,1,0:T(8,128)(2,1)S(1)} copy(bf16[16,8,16,128]{3,1,2,0:T(8,128)(2,1)} %bitcast.81) | data formatting | bytes 1048576
  46.4 0.1 copy.19
  47.3 0.4 broadcast_compare_fusion
  47.6 0.0 all-to-all-done
  47.7 1.3 %gather_fusion.1 = bf16[2,2,128,256]{3,2,1,0:T(8,128)(2,1)} fusion(bf16[4,2,128,256]{3,2,1,0:T(8,128)(2,1)S(1)} %all-to-all-done, s32[1024]{0:T(1024)S(1)} %pad_clamp_fusion), kind=kCustom, calls=%fused_computation.1 | custom fusion | bytes 524296 | tf_op jit(solution)/shard_map/gather | solution.py:105
  48.9 0.0 all-gather.3.cloned.1.call-update
  48.9 1.0 %fusion.14 = (f32[2,1024]{1,0:T(2,128)S(1)}, f32[2,1024,512]{1,2,0:T(8,128)S(1)}) fusion(pred[1024,512]{0,1:T(8,128)(4,1)S(1)} %broadcast_compare_fusion, bf16[2,1024,128]{2,1,0:T(8,128)(2,1)S(1)} %bitcast.72, bf16[2,512,256]{2,1,0:T(8,128)(2,1)S(1)} %bitcast.79), kind=kOutput, calls=%fused_computation.20 | convolution fusion | flops 271579136 | bytes 5513216 | tf_op jit(solution)/shard_map/while/body/eval_jaxpr/gqd,gkd->gqk/dot_general | solution.py:22
  49.9 1.1 %fusion.16 = f32[2,1024]{1,0:T(2,128)S(1)} fusion(f32[2,1024,512]{1,2,0:T(8,128)S(1)} %get-tuple-element.92, f32[2,1024]{1,0:T(2,128)S(1)} %broadcast_maximum_fusion, pred[1024,512]{0,1:T(8,128)(4,1)S(1)} %broadcast_compare_fusion), kind=kLoop, calls=%fused_computation.22 | loop fusion | flops 5240832 | bytes 4734976 | tf_op jit(solution)/shard_map/while/body/eval_jaxpr/reduce_sum | solution.py:31
  51.1 1.8 %fusion.20 = f32[2,1024,128]{2,1,0:T(8,128)S(1)} fusion(f32[2,1024,512]{1,2,0:T(8,128)S(1)} %get-tuple-element.92, f32[2,1024]{1,0:T(2,128)S(1)} %broadcast_maximum_fusion, pred[1024,512]{0,1:T(8,128)(4,1)S(1)} %broadcast_compare_fusion, f32[2,1024]{1,0:T(2,128)S(1)} %get-tuple-element.89, bf16[2,512,256]{2,1,0:T(8,128)(2,1)S(1)} %bitcast.80), kind=kOutput, calls=%fused_computation.25 | convolution fusion | flops 273940480 | bytes 6045696 | tf_op jit(solution)/shard_map/while/body/eval_jaxpr/gqk,gkd->gqd/dot_general | solution.py:32
  52.9 25.0 %all-gather.3.cloned.1.call-done = bf16[8,2,128,256]{3,2,1,0:T(8,128)(2,1)} async-done(((bf16[2,2,128,256]{3,2,1,0:T(8,128)(2,1)}), bf16[8,2,128,256]{3,2,1,0:T(8,128)(2,1)}) %all-gather.3.cloned.1.call-update) | async-done | bytes 1048592 | tf_op jit(solution)/shard_map/all_gather | solution.py:108
  77.9 1.3 %copy.22 = bf16[2,2,4,128,256]{4,3,2,1,0:T(8,128)(2,1)S(1)} copy(bf16[2,2,4,128,256]{4,3,1,2,0:T(8,128)(2,1)} %bitcast.78) | data formatting | bytes 2097152 | tf_op jit(solution)/shard_map/transpose | solution.py:114
  79.2 5.9 %while.2 = (s32[]{:T(128)}, f32[2,1024]{1,0:T(2,128)S(1)}, f32[2,1024]{1,0:T(2,128)S(1)}, f32[2,1024,128]{2,1,0:T(8,128)S(1)}, bf16[2,2,512,256]{3,2,1,0:T(8,128...) while((s32[]{:T(128)}, f32[2,1024]{1,0:T(2,128)S(1)}, f32[2,1024]{1,0:T(2,128)S(1)}, ...), condition=%wide.region_14.15_spmd, body=%wide.region_11.14_spmd.sunk | while | flops 545787904 | bytes 16908376 | solution.py:124
  79.2 0.7 bitcast_reduce_fusion.2
  80.0 0.7 fusion.57
  80.7 1.4 %fusion.58 = f32[2,1024,128]{2,1,0:T(8,128)S(1)} fusion(f32[2,512,1024]{2,1,0:T(8,128)S(1)} %get-tuple-element.137, f32[2,1024]{1,0:T(2,128)S(1)} %max.21, f32[2,1024,128]{2,1,0:T(8,128)S(1)} %get-tuple-element.150, f32[2,1024]{1,0:T(2,128)S(1)} %get-tuple-element.139, bf16[2,512,256]{2,1,0:T(8,128)(2,1)S(1)} %dynamic-slice_bitcast_fusion.2), kind=kOutput, calls=%fused_computation.10.clone.1 | convolution fusion | flops 272105472 | bytes 6569984 | tf_op jit(solution)/shard_map/while/body/eval_jaxpr/gqk,gkd->gqd/dot_general | solution.py:32
  82.2 0.7 bitcast_reduce_fusion.2
  82.9 0.7 fusion.57
  83.7 1.4 %fusion.58 = f32[2,1024,128]{2,1,0:T(8,128)S(1)} fusion(f32[2,512,1024]{2,1,0:T(8,128)S(1)} %get-tuple-element.137, f32[2,1024]{1,0:T(2,128)S(1)} %max.21, f32[2,1024,128]{2,1,0:T(8,128)S(1)} %get-tuple-element.150, f32[2,1024]{1,0:T(2,128)S(1)} %get-tuple-element.139, bf16[2,512,256]{2,1,0:T(8,128)(2,1)S(1)} %dynamic-slice_bitcast_fusion.2), kind=kOutput, calls=%fused_computation.10.clone.1 | convolution fusion | flops 272105472 | bytes 6569984 | tf_op jit(solution)/shard_map/while/body/eval_jaxpr/gqk,gkd->gqd/dot_general | solution.py:32
  85.1 0.3 divide_convert_fusion
  85.4 0.3 copy.23
  85.8 0.9 copy.29
  (22 shorter events, 0.3 us)
Async XLA Ops:
  14.1 33.5 %all-to-all-start = ((bf16[4,2,128,256]{3,2,1,0:T(8,128)(2,1)}), bf16[4,2,128,256]{3,2,1,0:T(8,128)(2,1)S(1)}, u32[]{:S(2)}, u32[]{:S(2)}) async-start(bf16[4,2,128,256]{3,2,1,0:T(8,128)(2,1)} %gather_fusion), calls=%async_computation | async-start | bytes 1048576 | tf_op jit(solution)/shard_map/all_to_all | solution.py:97
  20.5 57.4 %all-gather.3.cloned.1.call-start = ((), (), s32[]{:S(2)}) async-start(), calls=%async_computation.1 | async-start | bytes 1310720 | tf_op jit(solution)/shard_map/all_gather | solution.py:108
Sparse Core Ops, SparseCore 0:
  49.1 28.7 all-gather.2
where the time goes:
time: 93.9 us; the launch traced here: 93.6 us
  waiting for transfers between devices  25 us (27%)
  blocking collectives  22.8 us (24%)
  between operations  14.2 us (15%)
  local copies, waits for them, and re-layouts  9.7 us (10%)
  other arithmetic  8.44 us (9%)
  matrix products  7.01 us (7%)
  starting transfers between devices  6.32 us (7%)
    all_gather x1, waiting for transfers between devices, local(): incoming = lax.all_gather(compact, 'blk', axis=0, tiled=True)  25 us
    all_gather x1, blocking collectives, local(): incoming = lax.all_gather(kv_new, 'blk', axis=0, tiled=True)  22.8 us
    all_to_all x1, starting transfers between devices, local(): lax.all_to_all(kv_cache[chosen], 'blk', split_axis=0, concat_axis=0, tile...  6.32 us
    dot_general x3, matrix products, attend(): jnp.einsum('gqk,gkd->gqd', weights.astype(jnp.bfloat16), entries[..., hea...  4.59 us
    gather x1, local copies, waits for them, and re-layouts, local(): kv_cache[chosen]  3.56 us
    unnamed x3, local copies, waits for them, and re-layouts  2.99 us
    reduce_sum x3, other arithmetic, attend(): totals = totals * factor + jnp.sum(weights, axis=2)  2.52 us
    dot_general x3, matrix products, attend(): jnp.einsum('gqd,gkd->gqk', queries, entries[..., :head_size], preferred_e...  2.42 us
  transfers between devices with their start and end apart: 2, of which 1 were waited for; matrix products, arithmetic and copies ran while one was open for 8% of the time, Pallas kernels for 0%

commit v1 on v0

--- a/solution.py
+++ b/solution.py
@@ -6,6 +6,22 @@
 
 PG = 2
 CAP = 4
+
+
+def pairwise_exchange(x, axis, split, join):
+    ways, here = (lax.axis_size(axis), lax.axis_index(axis))
+    width = x.shape[split] // ways
+    shape = list(x.shape)
+    shape[split] = width
+    height = shape[join]
+    shape[join] = height * ways
+    full = jnp.zeros(shape, x.dtype)
+    for mask in range(ways):
+        part = lax.dynamic_slice_in_dim(x, (here ^ mask) * width, width, axis=split)
+        if mask:
+            part = lax.ppermute(part, axis, [(d, d ^ mask) for d in range(ways)])
+        full = lax.dynamic_update_slice_in_dim(full, part, (here ^ mask) * height, axis=join)
+    return full
 
 
 def divisor_below(total_count, upper_limit):
@@ -94,7 +110,7 @@
     wanted = (block_ids[:, None] - my_start) % blocks + peer_slots * blocks
     picked = owned[None, None, :] & (page_rank[None, None, :] == wanted[..., None])
     chosen = jnp.sum(jnp.where(picked, local_slot[None, None, :], 0), axis=2).reshape(-1)
-    received = lax.all_to_all(kv_cache[chosen], "blk", split_axis=0, concat_axis=0, tiled=True)
+    received = pairwise_exchange(kv_cache[chosen], "blk", 0, 0)
     arriving = (myself - starts[:, None]) % blocks + peer_slots * blocks
     present = (arriving < counts[:, None]).reshape(-1)
     order_rank = jnp.cumsum(present.astype(jnp.int32)) - 1

time: 93.9 us -> 87.8 us (0.935)
  blocking collectives: 22.8 us -> 19.1 us
  waiting for transfers between devices: 25 us -> 23.6 us
  local copies, waits for them, and re-layouts: 9.7 us -> 8.72 us
    all_to_all x1 -> x0, starting transfers between devices: 6.32 us -> none  [local(): lax.all_to_all(kv_cache[chosen], 'blk', split_axis=0, concat_axis=0, tile...]
    ppermute x0 -> x3, starting transfers between devices: none -> 5.62 us  [pairwise_exchange(): part = lax.ppermute(part, axis, [(d, d ^ mask) for d in range(ways)])]
    all_gather x1, blocking collectives: 22.8 us -> 19.1 us  [local(): incoming = lax.all_gather(kv_new, 'blk', axis=0, tiled=True)]
    all_gather x1, waiting for transfers between devices: 25 us -> 23.6 us  [local(): incoming = lax.all_gather(compact, 'blk', axis=0, tiled=True)]
    select_n x1, other arithmetic: 0.65 us -> 2 us  [local(): wanted = (block_ids[:, None] - my_start) % blocks + peer_slots * blocks]
    unnamed x3 -> x5, local copies, waits for them, and re-layouts: 2.99 us -> 1.96 us
  transfers between devices with their start and end apart: 2 -> 4, of which waited for: 1 -> 1; matrix products, arithmetic and copies ran while one was open for 8% -> 8% of each run, Pallas kernels for 0% -> 0%
where the time goes in v1:
time: 87.8 us; the launch traced here: 87.5 us
  waiting for transfers between devices  23.6 us (27%)
  blocking collectives  19.1 us (22%)
  between operations  14.2 us (16%)
  other arithmetic  9.11 us (10%)
  local copies, waits for them, and re-layouts  8.72 us (10%)
  matrix products  7.02 us (8%)
  starting transfers between devices  5.62 us (6%)
    all_gather x1, waiting for transfers between devices, local(): incoming = lax.all_gather(compact, 'blk', axis=0, tiled=True)  23.6 us
    all_gather x1, blocking collectives, local(): incoming = lax.all_gather(kv_new, 'blk', axis=0, tiled=True)  19.1 us
    ppermute x3, starting transfers between devices, pairwise_exchange(): part = lax.ppermute(part, axis, [(d, d ^ mask) for d in range(ways)])  5.62 us
    dot_general x3, matrix products, attend(): jnp.einsum('gqk,gkd->gqd', weights.astype(jnp.bfloat16), entries[..., hea...  4.59 us
    gather x1, local copies, waits for them, and re-layouts, local(): received = pairwise_exchange(kv_cache[chosen], 'blk', 0, 0)  2.77 us
    reduce_sum x3, other arithmetic, attend(): totals = totals * factor + jnp.sum(weights, axis=2)  2.52 us
    dot_general x3, matrix products, attend(): jnp.einsum('gqd,gkd->gqk', queries, entries[..., :head_size], preferred_e...  2.42 us
    select_n x1, other arithmetic, local(): wanted = (block_ids[:, None] - my_start) % blocks + peer_slots * blocks  2 us
  transfers between devices with their start and end apart: 4, of which 1 were waited for; matrix products, arithmetic and copies ran while one was open for 8% of the time, Pallas kernels for 0%

profile of v1, /device:TPU:0, one launch (start us, length us, event | category | flops | bytes accessed | tf_op | source)
XLA Modules:
  0.0 87.5 jit_solution(3879213225757134338)
XLA Ops:
  6.5 0.0 copy-start
  6.5 0.0 all-gather.3.cloned.1.call-start
  6.5 0.7 and_select_fusion.3
  7.3 0.7 convert_bitcast_fusion
  7.9 0.2 reduce-window.21
  8.1 0.1 convert_reduce_fusion
  8.2 0.2 reduce-window.22
  8.4 0.6 fusion.37
  9.1 2.0 %and_select_fusion.4 = (s32[4]{0:T(128)S(1)}, s32[]{:T(128)}) fusion(s32[]{:T(128)} %fusion.37, s32[4]{0:T(128)} %param.11, s32[]{:T(128)S(6)} %axis_index.19), kind=kLoop, calls=%fused_computation.74 | loop fusion | flops 59 | bytes 44 | tf_op jit(solution)/shard_map/jit(remainder)/select_n | solution.py:110
  11.0 0.2 select_reduce_fusion.1
  11.3 2.8 %gather_fusion = bf16[4,2,128,256]{3,2,1,0:T(8,128)(2,1)S(1)} fusion(bf16[32,2,128,256]{3,2,1,0:T(8,128)(2,1)} %param.9, s32[1024]{0:T(1024)S(1)} %pad_clamp_fusion.1), kind=kCustom, calls=%fused_computation | custom fusion | bytes 1048592 | tf_op jit(solution)/shard_map/gather | solution.py:113
  14.1 0.8 constant_dynamic-slice_fusion
  14.9 5.0 %collective-permute-start.2 = (bf16[1,2,128,256]{3,2,1,0:T(8,128)(2,1)}, bf16[1,2,128,256]{3,2,1,0:T(8,128)(2,1)S(1)}, u32[]{:S(2)}, u32[]{:S(2)}) collective-permute-start(bf16[1,2,128,256]{3,2,1,0:T(8,128)(2,1)} %get-tuple-element.89), channel_id=1, source_target_pairs={{0,12},{4,8},{8,4},{12,0},{1,13},{5,9},{9,5},{13,1},{2,14},{6,10},... | collective-permute-start | bytes 393224 | tf_op jit(solution)/shard_map/ppermute | solution.py:22
  19.9 0.0 collective-permute-start.1
  19.9 0.6 collective-permute-start
  20.5 0.2 reduce-window.23
  20.7 0.1 fusion.34
  21.5 0.7 select_reduce_fusion
  22.2 0.9 %copy.30 = bf16[128,2,256]{2,0,1:T(8,128)(2,1)S(1)} copy(bf16[128,2,256]{2,1,0:T(2,128)(2,1)} %param.8) | data formatting | bytes 262144 | tf_op args[1]
  23.1 0.4 broadcast_compare_fusion
  23.5 19.1 %all_gather.6 = bf16[512,2,256]{2,0,1:T(8,128)(2,1)S(1)} all-gather(bf16[128,2,256]{2,0,1:T(8,128)(2,1)S(1)} %copy.30), channel_id=1, replica_groups=mesh['groups'=2,'blk'=4,'pool'=4] {'blk'}, dimensions={0}, use_global_device_ids=true | all-gather | bytes 655360 | tf_op jit(solution)/shard_map/all_gather | solution.py:81
  42.6 0.0 copy-done
  42.6 0.1 copy.36
  42.7 0.1 copy.29
  42.9 0.0 collective-permute-done
  42.9 0.0 collective-permute-done.1
  43.0 0.0 collective-permute-done.2
  43.0 1.3 %gather_fusion.1 = bf16[2,2,128,256]{3,2,1,0:T(8,128)(2,1)} fusion(bf16[4,2,128,256]{3,2,1,0:T(8,128)(2,1)S(1)} %constant_dynamic-update-slice_fusion, s32[1024]{0:T(1024)S(1)} %pad_clamp_fusion), kind=kCustom, calls=%fused_computation.1 | custom fusion | bytes 524296 | tf_op jit(solution)/shard_map/gather | solution.py:121
  44.3 0.0 all-gather.3.cloned.1.call-update
  44.3 1.0 %fusion.14 = (f32[2,1024]{1,0:T(2,128)S(1)}, f32[2,1024,512]{1,2,0:T(8,128)S(1)}) fusion(pred[1024,512]{0,1:T(8,128)(4,1)S(1)} %broadcast_compare_fusion, bf16[2,1024,128]{2,1,0:T(8,128)(2,1)S(1)} %bitcast.72, bf16[2,512,256]{2,1,0:T(8,128)(2,1)S(1)} %bitcast.79), kind=kOutput, calls=%fused_computation.20 | convolution fusion | flops 271579136 | bytes 5513216 | tf_op jit(solution)/shard_map/while/body/eval_jaxpr/gqd,gkd->gqk/dot_general | solution.py:38
  45.3 1.1 %fusion.16 = f32[2,1024]{1,0:T(2,128)S(1)} fusion(f32[2,1024,512]{1,2,0:T(8,128)S(1)} %get-tuple-element.96, f32[2,1024]{1,0:T(2,128)S(1)} %broadcast_maximum_fusion, pred[1024,512]{0,1:T(8,128)(4,1)S(1)} %broadcast_compare_fusion), kind=kLoop, calls=%fused_computation.22 | loop fusion | flops 5240832 | bytes 4734976 | tf_op jit(solution)/shard_map/while/body/eval_jaxpr/reduce_sum | solution.py:47
  46.4 1.8 %fusion.20 = f32[2,1024,128]{2,1,0:T(8,128)S(1)} fusion(f32[2,1024,512]{1,2,0:T(8,128)S(1)} %get-tuple-element.96, f32[2,1024]{1,0:T(2,128)S(1)} %broadcast_maximum_fusion, pred[1024,512]{0,1:T(8,128)(4,1)S(1)} %broadcast_compare_fusion, f32[2,1024]{1,0:T(2,128)S(1)} %get-tuple-element.93, bf16[2,512,256]{2,1,0:T(8,128)(2,1)S(1)} %bitcast.80), kind=kOutput, calls=%fused_computation.25 | convolution fusion | flops 273940480 | bytes 6045696 | tf_op jit(solution)/shard_map/while/body/eval_jaxpr/gqk,gkd->gqd/dot_general | solution.py:48
  48.2 23.6 %all-gather.3.cloned.1.call-done = bf16[8,2,128,256]{3,2,1,0:T(8,128)(2,1)} async-done(((bf16[2,2,128,256]{3,2,1,0:T(8,128)(2,1)}), bf16[8,2,128,256]{3,2,1,0:T(8,128)(2,1)}) %all-gather.3.cloned.1.call-update) | async-done | bytes 1048592 | tf_op jit(solution)/shard_map/all_gather | solution.py:124
  71.8 1.3 %copy.32 = bf16[2,2,4,128,256]{4,3,2,1,0:T(8,128)(2,1)S(1)} copy(bf16[2,2,4,128,256]{4,3,1,2,0:T(8,128)(2,1)} %bitcast.78) | data formatting | bytes 2097152 | tf_op jit(solution)/shard_map/transpose | solution.py:130
  73.1 5.9 %while.2 = (s32[]{:T(128)}, f32[2,1024]{1,0:T(2,128)S(1)}, f32[2,1024]{1,0:T(2,128)S(1)}, f32[2,1024,128]{2,1,0:T(8,128)S(1)}, bf16[2,2,512,256]{3,2,1,0:T(8,128...) while((s32[]{:T(128)}, f32[2,1024]{1,0:T(2,128)S(1)}, f32[2,1024]{1,0:T(2,128)S(1)}, ...), condition=%wide.region_14.15_spmd, body=%wide.region_11.14_spmd.sunk | while | flops 545787904 | bytes 16908376 | solution.py:140
  73.2 0.7 bitcast_reduce_fusion.2
  73.9 0.7 fusion.57
  74.6 1.4 %fusion.58 = f32[2,1024,128]{2,1,0:T(8,128)S(1)} fusion(f32[2,512,1024]{2,1,0:T(8,128)S(1)} %get-tuple-element.141, f32[2,1024]{1,0:T(2,128)S(1)} %max.21, f32[2,1024,128]{2,1,0:T(8,128)S(1)} %get-tuple-element.154, f32[2,1024]{1,0:T(2,128)S(1)} %get-tuple-element.143, bf16[2,512,256]{2,1,0:T(8,128)(2,1)S(1)} %dynamic-slice_bitcast_fusion.2), kind=kOutput, calls=%fused_computation.10.clone.1 | convolution fusion | flops 272105472 | bytes 6569984 | tf_op jit(solution)/shard_map/while/body/eval_jaxpr/gqk,gkd->gqd/dot_general | solution.py:48
  76.1 0.7 bitcast_reduce_fusion.2
  76.9 0.7 fusion.57
  77.6 1.4 %fusion.58 = f32[2,1024,128]{2,1,0:T(8,128)S(1)} fusion(f32[2,512,1024]{2,1,0:T(8,128)S(1)} %get-tuple-element.141, f32[2,1024]{1,0:T(2,128)S(1)} %max.21, f32[2,1024,128]{2,1,0:T(8,128)S(1)} %get-tuple-element.154, f32[2,1024]{1,0:T(2,128)S(1)} %get-tuple-element.143, bf16[2,512,256]{2,1,0:T(8,128)(2,1)S(1)} %dynamic-slice_bitcast_fusion.2), kind=kOutput, calls=%fused_computation.10.clone.1 | convolution fusion | flops 272105472 | bytes 6569984 | tf_op jit(solution)/shard_map/while/body/eval_jaxpr/gqk,gkd->gqd/dot_general | solution.py:48
  79.0 0.3 divide_convert_fusion
  79.4 0.3 copy.33
  79.7 0.9 %copy.39 = bf16[16,8,16,128]{3,1,2,0:T(8,128)(2,1)} copy(bf16[16,8,16,128]{3,2,1,0:T(8,128)(2,1)S(1)} %bitcast.76) | data formatting | bytes 1048576
  (26 shorter events, 0.3 us)
Async XLA Ops:
  6.5 36.1 %copy-start = (bf16[128,2048]{1,0:T(8,128)(2,1)S(1)}, bf16[128,2048]{1,0:T(8,128)(2,1)}, u32[]{:S(2)}) copy-start(bf16[128,2048]{1,0:T(8,128)(2,1)} %param.7) | copy-start | bytes 1572868
  6.5 65.2 %all-gather.3.cloned.1.call-start = ((), (), s32[]{:S(2)}) async-start(), calls=%async_computation | async-start | bytes 1310720 | tf_op jit(solution)/shard_map/all_gather | solution.py:124
  14.9 28.1 %collective-permute-start.2 = (bf16[1,2,128,256]{3,2,1,0:T(8,128)(2,1)}, bf16[1,2,128,256]{3,2,1,0:T(8,128)(2,1)S(1)}, u32[]{:S(2)}, u32[]{:S(2)}) collective-permute-start(bf16[1,2,128,256]{3,2,1,0:T(8,128)(2,1)} %get-tuple-element.89), channel_id=1, source_target_pairs={{0,12},{4,8},{8,4},{12,0},{1,13},{5,9},{9,5},{13,1},{2,14},{6,10},... | collective-permute-start | bytes 393224 | tf_op jit(solution)/shard_map/ppermute | solution.py:22
  19.9 23.0 %collective-permute-start.1 = (bf16[1,2,128,256]{3,2,1,0:T(8,128)(2,1)}, bf16[1,2,128,256]{3,2,1,0:T(8,128)(2,1)S(1)}, u32[]{:S(2)}, u32[]{:S(2)}) collective-permute-start(bf16[1,2,128,256]{3,2,1,0:T(8,128)(2,1)} %get-tuple-element.90), channel_id=1, source_target_pairs={{0,8},{4,12},{8,0},{12,4},{1,9},{5,13},{9,1},{13,5},{2,10},{6,14},... | collective-permute-start | bytes 393224 | tf_op jit(solution)/shard_map/ppermute | solution.py:22
  19.9 23.0 %collective-permute-start = (bf16[1,2,128,256]{3,2,1,0:T(8,128)(2,1)}, bf16[1,2,128,256]{3,2,1,0:T(8,128)(2,1)S(1)}, u32[]{:S(2)}, u32[]{:S(2)}) collective-permute-start(bf16[1,2,128,256]{3,2,1,0:T(8,128)(2,1)} %get-tuple-element.91), channel_id=1, source_target_pairs={{0,4},{4,0},{8,12},{12,8},{1,5},{5,1},{9,13},{13,9},{2,6},{6,2},{1... | collective-permute-start | bytes 393224 | tf_op jit(solution)/shard_map/ppermute | solution.py:22
Sparse Core Ops, SparseCore 0:
  44.4 27.3 all-gather.2
